TPU v7x, 32 devices: a whole 2x2x4 slice. The times are simulated.
32 devices in a mesh: seq: 8 (over z, x), dp: 4 (over y, core).
Axes of the slice: x: 2, y: 2, z: 4, core: 2. Of those that a mesh axis runs over, the one named last changes fastest.
Arguments:
- encoder_out: bfloat16 [4, 2560, 1536], P('dp', 'seq'), may hold values from -0.59765625 to 0.59765625
- out_grad: bfloat16 [4, 2560, 1536], P('dp', 'seq'), may hold values from -12 to 12
- segment_states: bfloat16 [4, 1024, 1536], P('dp', 'seq'), may hold values from -6 to 6
- segment_starts: int32 [4, 1024], P('dp', 'seq'), may hold values from 0 to 320, as said below
- segment_counts: int32 [4, 8], P('dp', 'seq'), may hold values from 32 to 128, as said below
- segment_probs: int32 [4, 1024], P('dp', 'seq'), may hold values from 0 to 65535, as said below
- query_weight: bfloat16 [1536, 1536], P('dp'), may hold values from -0.15625 to 0.15625
- key_weight: bfloat16 [1536, 1536], P('dp'), may hold values from -0.15625 to 0.15625
Outputs:
- x_grad: bfloat16 [4, 2560, 1536], P('dp', 'seq')
- segment_grad: bfloat16 [4, 1024, 1536], P('dp', 'seq')
Inputs may be any that keep to these rules, and one draw needn't show every extreme that they name: `segment_starts`: for block s of sequence b, the entries s * 128 + j with j < segment_counts[b, s] hold distinct increasing local positions below 320 at which segments start; the other entries hold 320. Byte 0 of every sequence starts a segment. `segment_counts`: every sequence has one block with exactly 128 segments and another with exactly a quarter of 128. `segment_probs`: A slot holds 0 exactly when it is past its block's count; slot 0 of every sequence holds 65535.
All inputs are finite; a program needn't handle non-finite values.
Results may differ from a plain program's by a relative error of at most 0.0049.
Values may be sent and summed in bfloat16 or wider, within the bound.
No kernel may reach another device: no remote copies, remote signals or barrier semaphores. Data moves between devices by JAX's collectives and lax.ppermute only.
A program may use at most 64 MiB of HBM per device.

v0:
```python
import jax
import jax.numpy as jnp
from jax import lax
from jax.sharding import PartitionSpec as P

prob_scale = 65536.0
norm_eps = 1e-06
exact = lax.Precision.HIGHEST
contract_last = (((1,), (1,)), ((), ()))
contract_first = (((0,), (0,)), ((), ()))


def shifted(block, axis, distance):
    devices = range(lax.axis_size(axis))
    route = [(i - distance, i) for i in devices if i - distance in devices]
    return lax.ppermute(block, axis, route)


def normalize_grad(vectors, scales, unit_grad):
    inner_prod = jnp.sum(vectors * unit_grad, axis=-1, keepdims=True)
    return scales * unit_grad - scales * scales * scales * inner_prod * vectors


def carry_from(log_keep, vectors, shard_index, from_lower):
    running_log = jnp.cumsum(log_keep)
    before = running_log - log_keep
    shard_order = jnp.arange(log_keep.shape[0])
    if from_lower:
        own_value = lax.dynamic_index_in_dim(before, shard_index, keepdims=False)
        selected = shard_order < shard_index
        log_gap = own_value - running_log
    else:
        own_value = lax.dynamic_index_in_dim(running_log, shard_index, keepdims=False)
        selected = shard_order > shard_index
        log_gap = before - own_value
    factor = jnp.where(selected, jnp.exp(jnp.where(selected, log_gap, 0.0)), 0.0)
    return jnp.dot(factor[None, :], vectors, precision=exact)


def per_device(
    encoder_out,
    out_grad,
    segment_states,
    segment_starts,
    segment_counts,
    segment_probs,
    query_weight,
    key_weight,
):
    token_rows = encoder_out[0]
    grad_rows = out_grad[0]
    token_count = token_rows.shape[0]
    slot_count = segment_states.shape[1]
    shard_index = lax.axis_index("seq")
    full_query, full_key = (
        lax.all_gather(query_weight, "dp", axis=0, tiled=True),
        lax.all_gather(key_weight, "dp", axis=0, tiled=True),
    )
    key_rows = jnp.dot(token_rows, full_key, preferred_element_type=jnp.float32)
    queries = jnp.dot(token_rows, full_query, preferred_element_type=jnp.float32)
    query_scale = lax.rsqrt(jnp.sum(queries * queries, axis=1, keepdims=True) + norm_eps)
    key_scale = lax.rsqrt(jnp.sum(key_rows * key_rows, axis=1, keepdims=True) + norm_eps)
    query_unit = queries * query_scale
    key_unit = key_rows * key_scale
    position = jnp.arange(token_count)
    later_rows = (shard_index > 0) | (position > 0)
    key_before = shifted(key_unit[token_count - 1 :], "seq", 1)
    key_prior = jnp.concatenate([key_before, key_unit[:-1]], axis=0)
    cosine = jnp.sum(query_unit * key_prior, axis=1)
    segment_total = segment_counts[0, 0]
    slot_index = jnp.arange(slot_count)
    slot_used = slot_index < segment_total
    start_pos = segment_starts[0]
    smoothing = jnp.where(slot_used, segment_probs[0].astype(jnp.float32) / prob_scale, 0.0)
    reached = slot_used[None, :] & (start_pos[None, :] <= position[:, None])
    member_id = jnp.sum(reached.astype(jnp.int32), axis=1) - 1
    membership = (member_id[:, None] == slot_index[None, :]).astype(jnp.float32)
    leading = (member_id < 0).astype(jnp.float32)
    starts = jnp.any(slot_used[None, :] & (start_pos[None, :] == position[:, None]), axis=1)
    running = jnp.cumsum(jnp.log(1.0 - smoothing))
    lower = slot_index[None, :] <= slot_index[:, None]
    decay_table = jnp.where(
        lower, jnp.exp(jnp.where(lower, running[:, None] - running[None, :], 0.0)), 0.0
    )
    weighted_states = smoothing[:, None] * segment_states[0].astype(jnp.float32)
    local_state = jnp.dot(decay_table, weighted_states, precision=exact)
    keep_all = jnp.exp(running)
    boundary_prob = jnp.where(later_rows, 0.5 * (1.0 - cosine), 1.0)
    confidence = jnp.where(starts, boundary_prob, 1.0 - boundary_prob)
    weighted_grad = confidence[:, None] * grad_rows
    slot_grad = lax.dot_general(membership, weighted_grad, contract_first, precision=exact)
    lead_grad = jnp.dot(leading[None, :], weighted_grad, precision=exact)
    back_vector = lead_grad + jnp.dot(keep_all[None, :], slot_grad, precision=exact)
    last_log = running[slot_count - 1 :]
    last_state = local_state[slot_count - 1 :]
    summaries = (
        lax.all_gather(last_log, "seq", axis=0, tiled=True),
        lax.all_gather(last_state, "seq", axis=0, tiled=True),
        lax.all_gather(last_log, "seq", axis=0, tiled=True),
        lax.all_gather(back_vector, "seq", axis=0, tiled=True),
    )
    state_in = carry_from(summaries[0], summaries[1], shard_index, True)
    grad_in = carry_from(summaries[2], summaries[3], shard_index, False)
    smoothed = local_state + keep_all[:, None] * state_in
    picked = jnp.dot(membership, smoothed, precision=exact) + leading[:, None] * state_in
    conf_grad = jnp.sum(grad_rows * picked, axis=1)
    cos_grad = jnp.where(later_rows, jnp.where(starts, -0.5 * conf_grad, 0.5 * conf_grad), 0.0)
    reach_end = jnp.exp(running[slot_count - 1] - running)
    state_grad = (
        lax.dot_general(decay_table, slot_grad, contract_first, precision=exact)
        + reach_end[:, None] * grad_in
    )
    segment_grad = (smoothing[:, None] * state_grad).astype(jnp.bfloat16)
    unit_q_grad = cos_grad[:, None] * key_prior
    prior_grad = cos_grad[:, None] * query_unit
    query_grad = normalize_grad(queries, query_scale, unit_q_grad).astype(jnp.bfloat16)
    from_next = shifted(prior_grad[:1], "seq", -1)
    unit_k_grad = jnp.concatenate([prior_grad[1:], from_next], axis=0)
    key_grad = normalize_grad(key_rows, key_scale, unit_k_grad).astype(jnp.bfloat16)
    x_grad = lax.dot_general(
        query_grad, full_query, contract_last, preferred_element_type=jnp.float32
    )
    x_grad = x_grad + lax.dot_general(
        key_grad, full_key, contract_last, preferred_element_type=jnp.float32
    )
    return (x_grad.astype(jnp.bfloat16)[None], segment_grad[None])


def solution(mesh):
    placed = (
        P("dp", "seq", None),
        P("dp", "seq", None),
        P("dp", "seq", None),
        P("dp", "seq"),
        P("dp", "seq"),
        P("dp", "seq"),
        P("dp", None),
        P("dp", None),
    )
    return jax.shard_map(
        per_device,
        mesh=mesh,
        in_specs=placed,
        out_specs=(P("dp", "seq", None), P("dp", "seq", None)),
        check_vma=False,
    )
```

profile of v0, /device:TPU:0, one launch (start us, length us, event | category | flops | bytes accessed | tf_op | source)
XLA Modules:
  0.0 151.8 jit_solution(7152754689850499982)
XLA Ops:
  7.3 0.7 all-gather.7.cloned.1.call-update
  8.0 0.7 all-gather.9.cloned.1.call-update
  9.7 0.6 slice.29
  10.3 0.6 dynamic-slice.2
  10.8 1.3 bitcast_dynamic-update-slice_fusion
  12.1 23.1 %all-reduce = f32[8]{0:T(128)S(1)} all-reduce(f32[8]{0:T(128)S(1)} %bitcast_dynamic-update-slice_fusion), channel_id=2, replica_groups=mesh['seq'=8,'dp'=4] {'seq'}, use_global_device_ids=true, to_apply=%add | all-reduce | flops 8 | bytes 64
  35.5 0.6 constant_dynamic-slice_fusion
  36.1 0.9 fusion.24
  37.0 30.7 %all-gather.2 = f32[8,1,1536]{2,1,0:T(1,128)S(1)} all-gather(f32[1,1,1536]{2,1,0:T(1,128)S(1)} %slice_bitcast_fusion), channel_id=1, replica_groups=mesh['seq'=8,'dp'=4] {'seq'}, dimensions={0}, use_global_device_ids=true | all-gather | bytes 55296 | tf_op jit(solution)/shard_map/all_gather | solution.py:98
  67.7 0.8 convolution_reduce_fusion.2
  68.9 0.6 subtract_exponential_fusion
  69.6 1.5 fusion.8
  71.1 4.2 %multiply_reduce_fusion.4 = (f32[320]{0:T(512)S(1)}, f32[320,1536]{1,0:T(8,128)S(1)}) fusion(bf16[1536,1536]{1,0:T(8,128)(2,1)} %all-gather.7.cloned.1.call-done, bf16[1,320,1536]{2,1,0:T(8,128)(2,1)S(1)} %copy-done), kind=kOutput, calls=%fused_computation.20 | convolution fusion | flops 1510932224 | bytes 7668992 | tf_op jit(solution)/shard_map/dot_general | solution.py:60
  75.2 0.3 multiply_multiply_fusion
  75.5 1.3 collective-permute-start.1
  76.8 1.4 slice.33
  78.3 10.6 %all-gather.9.cloned.1.call-done = bf16[1536,1536]{1,0:T(8,128)(2,1)} async-done(((bf16[384,1536]{1,0:T(8,128)(2,1)}), bf16[1536,1536]{1,0:T(8,128)(2,1)}) %all-gather.9.cloned.1.call-update) | async-done | bytes 4718608 | tf_op jit(solution)/shard_map/all_gather | solution.py:57
  88.9 4.8 %multiply_reduce_fusion.1 = (f32[320]{0:T(512)S(1)}, f32[320]{0:T(512)S(1)}, f32[320,1536]{1,0:T(8,128)S(1)}) fusion(f32[1,1536]{1,0:T(1,128)S(1)} %collective-permute-done.1, f32[319,1536]{1,0:T(8,128)} %slice.33, bf16[1536,1536]{1,0:T(8,128)(2,1)} %all-gather.9.cloned.1.call-done, bf16[1,320,1536]{2,1,0:T(8,128)(2,1)S(1)} %copy-done), kind=kOutput, calls=%fused_computation.16 | convolution fusion | flops 1512406528 | bytes 9636352 | tf_op jit(solution)/shard_map/dot_general | solution.py:59
  93.7 0.2 broadcast_multiply_fusion
  93.9 3.4 %collective-permute-start = (f32[1,1536]{1,0:T(1,128)S(1)}, f32[1,1536]{1,0:T(1,128)S(1)}, u32[]{:S(2)}, u32[]{:S(2)}) collective-permute-start(f32[1,1536]{1,0:T(1,128)S(1)} %slice.31), channel_id=1, source_target_pairs={{0,4},{4,8},{8,12},{12,16},{16,20},{20,24},{24,28},{1,5},{5,9},{9,... | collective-permute-start | bytes 18440 | tf_op jit(solution)/shard_map/ppermute | solution.py:16
  97.3 0.6 constant_dynamic-slice_fusion.1
  97.9 0.7 collective-permute-done
  98.7 0.8 multiply_reduce_fusion
  99.5 0.4 copy-done.2
  99.9 1.2 fusion.7
  101.1 0.9 fusion.9
  102.0 0.5 convolution_reduce_fusion
  102.6 32.6 %all-gather.3 = f32[8,1,1536]{2,1,0:T(1,128)S(1)} all-gather(f32[1,1,1536]{2,1,0:T(1,128)S(1)} %reshape.174), channel_id=3, replica_groups=mesh['seq'=8,'dp'=4] {'seq'}, dimensions={0}, use_global_device_ids=true | all-gather | bytes 55296 | tf_op jit(solution)/shard_map/all_gather | solution.py:100
  135.2 0.8 convolution_reduce_fusion.1
  136.0 1.7 %fusion.5 = bf16[1,128,1536]{2,1,0:T(8,128)(2,1)} fusion(f32[128,1536]{1,0:T(8,128)S(1)} %fusion.7, f32[1536]{0:T(1024)S(1)} %convolution_reduce_fusion.1, f32[128]{0:T(128)S(1)} %get-tuple-element.10, f32[128]{0:T(128)S(1)} %bitcast_select_fusion, f32[128]{0:T(128)S(1)} %reduce), kind=kOutput, calls=%fused_computation.9 | convolution fusion | flops 302841856 | bytes 1187328 | tf_op jit(solution)/shard_map/dot_general | solution.py:110
  137.7 4.3 %fusion.10 = f32[320,1536]{1,0:T(8,128)S(1)} fusion(bf16[1536,1536]{1,0:T(8,128)(2,1)} %all-gather.7.cloned.1.call-done, f32[320,1536]{1,0:T(8,128)S(1)} %get-tuple-element.13, f32[319,1536]{1,0:T(8,128)S(1)} %bitcast.85, f32[1,1536]{1,0:T(1,128)S(1)} %collective-permute-done, f32[320]{0:T(512)S(1)} %get-tuple-element.16, f32[320]{0:T(512)S(1)} %select_select_fusion, ...), kind=kOutput, calls=%fused_computation.27 | convolution fusion | flops 1512898560 | bytes 10620672 | tf_op jit(solution)/shard_map/dot_general | solution.py:120
  142.1 2.9 %fusion.2 = bf16[1,320,1536]{2,1,0:T(8,128)(2,1)} fusion(f32[320,1536]{1,0:T(8,128)S(1)} %fusion.10, bf16[1536,1536]{1,0:T(8,128)(2,1)S(1)} %bitcast.89, f32[320,1536]{1,0:T(8,128)S(1)} %get-tuple-element.14, f32[1,1536]{1,0:T(1,128)S(1)} %collective-permute-done.1, f32[319,1536]{1,0:T(8,128)S(1)} %copy-done.3, f32[320]{0:T(512)S(1)} %get-tuple-element.8, ...), kind=kOutput, calls=%fused_computation.4 | convolution fusion | flops 1513390080 | bytes 11602432 | tf_op jit(solution)/shard_map/dot_general | solution.py:123
  (47 shorter events, 1.1 us)
Async XLA Ops:
  7.2 63.9 %copy-start = (bf16[1,320,1536]{2,1,0:T(8,128)(2,1)S(1)}, bf16[1,320,1536]{2,1,0:T(8,128)(2,1)}, u32[]{:S(2)}) copy-start(bf16[1,320,1536]{2,1,0:T(8,128)(2,1)} %param.8) | copy-start | bytes 2949124
  7.2 3.1 %copy-start.7 = (u32[32]{0:T(128)S(1)}, u32[32]{0:T(128)}, u32[]{:S(2)}) copy-start(u32[32]{0:T(128)} %constant.53) | copy-start | bytes 388
  7.2 2.2 %copy-start.6 = (s32[1,128]{1,0:T(1,128)S(1)}, s32[1,128]{1,0:T(1,128)}, u32[]{:S(2)}) copy-start(s32[1,128]{1,0:T(1,128)} %param.13) | copy-start | bytes 1540
  7.2 28.9 %copy-start.4 = (bf16[1,128,1536]{2,1,0:T(8,128)(2,1)S(1)}, bf16[1,128,1536]{2,1,0:T(8,128)(2,1)}, u32[]{:S(2)}) copy-start(bf16[1,128,1536]{2,1,0:T(8,128)(2,1)} %param.10) | copy-start | bytes 1179652
  7.2 61.4 %copy-start.5 = (s32[1,128]{1,0:T(1,128)S(1)}, s32[1,128]{1,0:T(1,128)}, u32[]{:S(2)}) copy-start(s32[1,128]{1,0:T(1,128)} %param.11) | copy-start | bytes 1540
  7.2 62.3 %copy-start.1 = (bf16[1,320,1536]{2,1,0:T(8,128)(2,1)S(1)}, bf16[1,320,1536]{2,1,0:T(8,128)(2,1)}, u32[]{:S(2)}) copy-start(bf16[1,320,1536]{2,1,0:T(8,128)(2,1)} %param.9) | copy-start | bytes 2949124
  7.2 63.8 %all-gather.7.cloned.1.call-start = ((), (), s32[]{:S(2)}) async-start(), calls=%async_computation | async-start | bytes 5898240 | tf_op jit(solution)/shard_map/all_gather | solution.py:56
  8.0 80.9 %all-gather.9.cloned.1.call-start = ((), (), s32[]{:S(2)}) async-start(), calls=%async_computation.1 | async-start | bytes 5898240 | tf_op jit(solution)/shard_map/all_gather | solution.py:57
  75.5 13.4 %collective-permute-start.1 = (f32[1,1536]{1,0:T(1,128)S(1)}, f32[1,1536]{1,0:T(1,128)S(1)}, u32[]{:S(2)}, u32[]{:S(2)}) collective-permute-start(f32[1,1536]{1,0:T(1,128)S(1)} %slice.34), channel_id=1, source_target_pairs={{4,0},{8,4},{12,8},{16,12},{20,16},{24,20},{28,24},{5,1},{9,5},{13... | collective-permute-start | bytes 18440 | tf_op jit(solution)/shard_map/ppermute | solution.py:16
  93.9 4.7 %collective-permute-start = (f32[1,1536]{1,0:T(1,128)S(1)}, f32[1,1536]{1,0:T(1,128)S(1)}, u32[]{:S(2)}, u32[]{:S(2)}) collective-permute-start(f32[1,1536]{1,0:T(1,128)S(1)} %slice.31), channel_id=1, source_target_pairs={{0,4},{4,8},{8,12},{12,16},{16,20},{20,24},{24,28},{1,5},{5,9},{9,... | collective-permute-start | bytes 18440 | tf_op jit(solution)/shard_map/ppermute | solution.py:16
  98.7 1.2 copy-start.2
  136.0 6.0 %slice-start = ((s8[4718592]{0:T(1024)(128)(4,1)}), s8[4194304]{0:T(1024)(128)(4,1)S(1)}, s32[]{:S(2)}) async-start(s8[4718592]{0:T(1024)(128)(4,1)} %bitcast.88), calls=%async_computation.2 | async-start | bytes 8388608
  137.7 4.4 %copy-start.3 = (f32[319,1536]{1,0:T(8,128)S(1)}, f32[319,1536]{1,0:T(8,128)}, u32[]{:S(2)}) copy-start(f32[319,1536]{1,0:T(8,128)} %slice.33) | copy-start | bytes 5879812
  137.7 4.4 %slice-start.1 = ((s8[4718592]{0:T(1024)(128)(4,1)}), s8[524288]{0:T(1024)(128)(4,1)S(1)}, s32[]{:S(2)}) async-start(s8[4718592]{0:T(1024)(128)(4,1)} %bitcast.88), calls=%async_computation.3 | async-start | bytes 1048576
Sparse Core Ops, SparseCore 0:
  9.6 40.1 all-gather.6
  51.4 37.4 all-gather.8
where the time goes:
time: 152 us
  blocking collectives  86.4 us (57%)
  matrix products  24.5 us (16%)
  between operations  15 us (10%)
  waiting for transfers between devices  12.7 us (8%)
  local copies, waits for them, and re-layouts  5.63 us (4%)
  starting transfers between devices  4.76 us (3%)
  other arithmetic  2.75 us (2%)
    all_gather x1, blocking collectives, per_device(): lax.all_gather(back_vector, 'seq', axis=0, tiled=True)  32.6 us
    all_gather x1, blocking collectives, per_device(): lax.all_gather(last_state, 'seq', axis=0, tiled=True)  30.7 us
    unnamed x1, blocking collectives  23.1 us
    all_gather x1, waiting for transfers between devices, per_device(): lax.all_gather(key_weight, 'dp', axis=0, tiled=True)  10.6 us
    dot_general x1, matrix products, per_device(): key_rows = jnp.dot(token_rows, full_key, preferred_element_type=jnp.float32)  4.83 us
    ppermute x2, starting transfers between devices, shifted(): return lax.ppermute(block, axis, route)  4.68 us
    dot_general x1, matrix products, per_device(): lax.dot_general(query_grad, full_query, contract_last, preferred_element_...  4.34 us
    dot_general x1, matrix products, per_device(): jnp.dot(token_rows, full_query, preferred_element_type=jnp.float32)  4.17 us
  transfers between devices with their start and end apart: 4, of which 2 were waited for; matrix products, arithmetic and copies ran while one was open for 9% of the time, Pallas kernels for 0%

commit v1 on v0

--- a/solution.py
+++ b/solution.py
@@ -8,6 +8,27 @@
 exact = lax.Precision.HIGHEST
 contract_last = (((1,), (1,)), ((), ()))
 contract_first = (((0,), (0,)), ((), ()))
+
+
+def joined_along(blocks, dim):
+    lengths = list(blocks.shape[1:])
+    lengths[dim] *= blocks.shape[0]
+    return jnp.moveaxis(blocks, 0, dim).reshape(lengths)
+
+
+def doubled(shard, axis):
+    count, mine = (lax.axis_size(axis), lax.axis_index(axis))
+    blocks, stride = (shard[None], 1)
+    while stride < count:
+        other = lax.ppermute(blocks, axis, [(i, i ^ stride) for i in range(count)])
+        low = mine & stride == 0
+        blocks = jnp.concatenate([jnp.where(low, blocks, other), jnp.where(low, other, blocks)])
+        stride *= 2
+    return blocks
+
+
+def gather_by_bits(x, axis, dim):
+    return joined_along(doubled(x, axis), dim)
 
 
 def shifted(block, axis, distance):
@@ -97,7 +118,7 @@
         lax.all_gather(last_log, "seq", axis=0, tiled=True),
         lax.all_gather(last_state, "seq", axis=0, tiled=True),
         lax.all_gather(last_log, "seq", axis=0, tiled=True),
-        lax.all_gather(back_vector, "seq", axis=0, tiled=True),
+        gather_by_bits(back_vector, "seq", 0),
     )
     state_in = carry_from(summaries[0], summaries[1], shard_index, True)
     grad_in = carry_from(summaries[2], summaries[3], shard_index, False)

time: 152 us -> 133 us (0.88)
  blocking collectives: 86.4 us -> 53.8 us
  starting transfers between devices: 4.76 us -> 12.9 us
  matrix products: 24.5 us -> 26.7 us
  waiting for transfers between devices: 12.7 us -> 14.4 us
    all_gather x1 -> x0, blocking collectives: 32.6 us -> none  [per_device(): lax.all_gather(back_vector, 'seq', axis=0, tiled=True)]
    ppermute x0 -> x3, starting transfers between devices: none -> 7.84 us  [doubled(): other = lax.ppermute(blocks, axis, [(i, i ^ stride) for i in range(count)])]
    dot_general x1, matrix products: 2.85 us -> 5.13 us  [per_device(): lax.dot_general(key_grad, full_key, contract_last, preferred_element_type...]
    unnamed x25 -> x34, local copies, waits for them, and re-layouts: 2.31 us -> 4.38 us
  transfers between devices with their start and end apart: 4 -> 7, of which waited for: 2 -> 3; matrix products, arithmetic and copies ran while one was open for 9% -> 17% of each run, Pallas kernels for 0% -> 0%
where the time goes in v1:
time: 133 us; the launch traced here: 132 us
  blocking collectives  53.8 us (40%)
  matrix products  26.7 us (20%)
  between operations  15.1 us (11%)
  waiting for transfers between devices  14.4 us (11%)
  starting transfers between devices  12.9 us (10%)
  local copies, waits for them, and re-layouts  6.44 us (5%)
  other arithmetic  2.95 us (2%)
    all_gather x1, blocking collectives, per_device(): lax.all_gather(last_state, 'seq', axis=0, tiled=True)  30.7 us
    unnamed x1, blocking collectives  23.1 us
    all_gather x1, waiting for transfers between devices, per_device(): lax.all_gather(key_weight, 'dp', axis=0, tiled=True)  10.8 us
    ppermute x3, starting transfers between devices, doubled(): other = lax.ppermute(blocks, axis, [(i, i ^ stride) for i in range(count)])  7.84 us
    dot_general x1, matrix products, per_device(): lax.dot_general(key_grad, full_key, contract_last, preferred_element_type...  5.13 us
    ppermute x2, starting transfers between devices, shifted(): return lax.ppermute(block, axis, route)  4.98 us
    dot_general x1, matrix products, per_device(): lax.dot_general(query_grad, full_query, contract_last, preferred_element_...  4.86 us
    unnamed x34, local copies, waits for them, and re-layouts  4.38 us
  transfers between devices with their start and end apart: 7, of which 3 were waited for; matrix products, arithmetic and copies ran while one was open for 17% of the time, Pallas kernels for 0%

profile of v1, /device:TPU:0, one launch (start us, length us, event | category | flops | bytes accessed | tf_op | source)
XLA Modules:
  0.0 132.2 jit_solution(12041642143235311803)
XLA Ops:
  7.3 0.7 all-gather.5.cloned.1.call-update
  8.0 0.7 all-gather.7.cloned.1.call-update
  9.7 0.6 slice.29
  10.3 0.6 dynamic-slice.2
  10.8 1.3 bitcast_dynamic-update-slice_fusion
  12.1 23.1 %all-reduce = f32[8]{0:T(128)S(1)} all-reduce(f32[8]{0:T(128)S(1)} %bitcast_dynamic-update-slice_fusion), channel_id=2, replica_groups=mesh['seq'=8,'dp'=4] {'seq'}, use_global_device_ids=true, to_apply=%add | all-reduce | flops 8 | bytes 64
  35.5 0.6 constant_dynamic-slice_fusion
  36.1 0.9 fusion.24
  37.0 30.7 %all-gather.1 = f32[8,1,1536]{2,1,0:T(1,128)S(1)} all-gather(f32[1,1,1536]{2,1,0:T(1,128)S(1)} %slice_bitcast_fusion), channel_id=1, replica_groups=mesh['seq'=8,'dp'=4] {'seq'}, dimensions={0}, use_global_device_ids=true | all-gather | bytes 55296 | tf_op jit(solution)/shard_map/all_gather | solution.py:119
  67.7 0.8 convolution_reduce_fusion.2
  68.9 0.6 subtract_exponential_fusion
  69.6 1.5 %fusion.8 = f32[320]{0:T(512)S(1)} fusion(bf16[1,320,1536]{2,1,0:T(8,128)(2,1)S(1)} %copy-done.5, f32[1536]{0:T(1024)S(1)} %convolution_reduce_fusion.2, f32[320]{0:T(512)S(1)} %get-tuple-element.6, f32[128,1536]{1,0:T(8,128)S(1)} %fusion.24, f32[128]{0:T(128)S(1)} %get-tuple-element.17, s32[320]{0:T(512)S(1)} %broadcast_add_fusion), kind=kOutput, calls=%fused_computation.22 | convolution fusion | flops 757866176 | bytes 1779968 | tf_op jit(solution)/shard_map/dot_general | solution.py:126
  71.1 4.2 %multiply_reduce_fusion.4 = (f32[320]{0:T(512)S(1)}, f32[320,1536]{1,0:T(8,128)S(1)}) fusion(bf16[1536,1536]{1,0:T(8,128)(2,1)} %all-gather.5.cloned.1.call-done, bf16[1,320,1536]{2,1,0:T(8,128)(2,1)S(1)} %copy-done), kind=kOutput, calls=%fused_computation.20 | convolution fusion | flops 1510932224 | bytes 7668992 | tf_op jit(solution)/shard_map/dot_general | solution.py:81
  75.5 1.1 copy-done.1
  76.6 1.3 collective-permute-start.1
  78.1 10.8 %all-gather.7.cloned.1.call-done = bf16[1536,1536]{1,0:T(8,128)(2,1)} async-done(((bf16[384,1536]{1,0:T(8,128)(2,1)}), bf16[1536,1536]{1,0:T(8,128)(2,1)}) %all-gather.7.cloned.1.call-update) | async-done | bytes 4718608 | tf_op jit(solution)/shard_map/all_gather | solution.py:78
  88.9 4.2 %multiply_reduce_fusion.1 = (f32[320]{0:T(512)S(1)}, f32[320]{0:T(512)S(1)}, f32[320,1536]{1,0:T(8,128)S(1)}) fusion(f32[1,1536]{1,0:T(1,128)S(1)} %collective-permute-done.1, f32[319,1536]{1,0:T(8,128)S(1)} %slice.33, bf16[1536,1536]{1,0:T(8,128)(2,1)} %all-gather.7.cloned.1.call-done, bf16[1,320,1536]{2,1,0:T(8,128)(2,1)S(1)} %copy-done), kind=kOutput, calls=%fused_computation.16 | convolution fusion | flops 1512406528 | bytes 9636352 | tf_op jit(solution)/shard_map/dot_general | solution.py:80
  93.3 1.0 copy-done.7
  94.3 3.7 %collective-permute-start = (f32[1,1536]{1,0:T(1,128)S(1)}, f32[1,1536]{1,0:T(1,128)S(1)}, u32[]{:S(2)}, u32[]{:S(2)}) collective-permute-start(f32[1,1536]{1,0:T(1,128)S(1)} %slice.31), channel_id=1, source_target_pairs={{0,4},{4,8},{8,12},{12,16},{16,20},{20,24},{24,28},{1,5},{5,9},{9,... | collective-permute-start | bytes 18440 | tf_op jit(solution)/shard_map/ppermute | solution.py:37
  98.1 1.1 collective-permute-done
  99.2 0.9 multiply_reduce_fusion
  100.4 1.2 fusion.7
  101.6 0.9 fusion.9
  103.1 2.4 %collective-permute-start.2 = (f32[1,1,1536]{2,1,0:T(1,128)S(1)}, f32[1,1,1536]{2,1,0:T(1,128)S(1)}, u32[]{:S(2)}, u32[]{:S(2)}) collective-permute-start(f32[1,1,1536]{2,1,0:T(1,128)S(1)} %broadcast_in_dim.69), channel_id=1, source_target_pairs={{0,4},{4,0},{8,12},{12,8},{16,20},{20,16},{24,28},{28,24},{1,5},{5... | collective-permute-start | bytes 18440 | tf_op jit(solution)/shard_map/ppermute | solution.py:23
  105.5 0.6 constant_dynamic-slice_fusion.1
  106.0 1.0 collective-permute-done.2
  107.1 3.0 %collective-permute-start.3 = (f32[2,1,1536]{2,1,0:T(1,128)S(1)}, f32[2,1,1536]{2,1,0:T(1,128)S(1)}, u32[]{:S(2)}, u32[]{:S(2)}) collective-permute-start(f32[2,1,1536]{2,1,0:T(1,128)S(1)} %pad_maximum_fusion.4), channel_id=1, source_target_pairs={{0,8},{4,12},{8,0},{12,4},{16,24},{20,28},{24,16},{28,20},{1,9},{5... | collective-permute-start | bytes 36872 | tf_op jit(solution)/shard_map/ppermute | solution.py:23
  110.1 4.9 %fusion.10 = f32[320,1536]{1,0:T(8,128)S(1)} fusion(bf16[1536,1536]{1,0:T(8,128)(2,1)} %all-gather.5.cloned.1.call-done, f32[320,1536]{1,0:T(8,128)} %copy-done.1, f32[319,1536]{1,0:T(8,128)S(1)} %bitcast.85, f32[1,1536]{1,0:T(1,128)S(1)} %collective-permute-done, f32[320]{0:T(512)S(1)} %get-tuple-element.22, f32[320]{0:T(512)S(1)} %select_select_fusion, ...), kind=kOutput, calls=%fused_computation.27 | convolution fusion | flops 1512898560 | bytes 10620672 | tf_op jit(solution)/shard_map/dot_general | solution.py:141
  115.0 2.5 %collective-permute-start.4 = (f32[4,1,1536]{2,1,0:T(1,128)S(1)}, f32[4,1,1536]{2,1,0:T(1,128)S(1)}, u32[]{:S(2)}, u32[]{:S(2)}) collective-permute-start(f32[4,1,1536]{2,1,0:T(1,128)S(1)} %pad_maximum_fusion.3), channel_id=1, source_target_pairs={{0,16},{4,20},{8,24},{12,28},{16,0},{20,4},{24,8},{28,12},{1,17},{... | collective-permute-start | bytes 73736 | tf_op jit(solution)/shard_map/ppermute | solution.py:23
  117.5 5.1 %fusion.2 = bf16[1,320,1536]{2,1,0:T(8,128)(2,1)} fusion(f32[320,1536]{1,0:T(8,128)S(1)} %fusion.10, bf16[1536,1536]{1,0:T(8,128)(2,1)} %all-gather.7.cloned.1.call-done, f32[320,1536]{1,0:T(8,128)S(1)} %copy-done.8, f32[1,1536]{1,0:T(1,128)S(1)} %collective-permute-done.1, f32[319,1536]{1,0:T(8,128)S(1)} %copy-done.10, f32[320]{0:T(512)S(1)} %get-tuple-element.14, ...), kind=kOutput, calls=%fused_computation.4 | convolution fusion | flops 1513390080 | bytes 11602432 | tf_op jit(solution)/shard_map/dot_general | solution.py:144
  122.8 0.8 convolution_reduce_fusion.1
  123.6 1.7 %fusion.5 = bf16[1,128,1536]{2,1,0:T(8,128)(2,1)} fusion(f32[128,1536]{1,0:T(8,128)S(1)} %copy-done.4, f32[1536]{0:T(1024)S(1)} %convolution_reduce_fusion.1, f32[128]{0:T(128)S(1)} %get-tuple-element.16, f32[128]{0:T(128)S(1)} %bitcast_select_fusion, f32[128]{0:T(128)S(1)} %reduce), kind=kOutput, calls=%fused_computation.9 | convolution fusion | flops 302841856 | bytes 1187328 | tf_op jit(solution)/shard_map/dot_general | solution.py:131
  (67 shorter events, 2.7 us)
Async XLA Ops:
  7.2 63.9 %copy-start = (bf16[1,320,1536]{2,1,0:T(8,128)(2,1)S(1)}, bf16[1,320,1536]{2,1,0:T(8,128)(2,1)}, u32[]{:S(2)}) copy-start(bf16[1,320,1536]{2,1,0:T(8,128)(2,1)} %param.8) | copy-start | bytes 2949124
  7.2 3.1 %copy-start.14 = (u32[32]{0:T(128)S(1)}, u32[32]{0:T(128)}, u32[]{:S(2)}) copy-start(u32[32]{0:T(128)} %constant.59) | copy-start | bytes 388
  7.2 2.2 %copy-start.13 = (s32[1,128]{1,0:T(1,128)S(1)}, s32[1,128]{1,0:T(1,128)}, u32[]{:S(2)}) copy-start(s32[1,128]{1,0:T(1,128)} %param.13) | copy-start | bytes 1540
  7.2 28.9 %copy-start.11 = (bf16[1,128,1536]{2,1,0:T(8,128)(2,1)S(1)}, bf16[1,128,1536]{2,1,0:T(8,128)(2,1)}, u32[]{:S(2)}) copy-start(bf16[1,128,1536]{2,1,0:T(8,128)(2,1)} %param.10) | copy-start | bytes 1179652
  7.2 61.4 %copy-start.12 = (s32[1,128]{1,0:T(1,128)S(1)}, s32[1,128]{1,0:T(1,128)}, u32[]{:S(2)}) copy-start(s32[1,128]{1,0:T(1,128)} %param.11) | copy-start | bytes 1540
  7.2 62.3 %copy-start.5 = (bf16[1,320,1536]{2,1,0:T(8,128)(2,1)S(1)}, bf16[1,320,1536]{2,1,0:T(8,128)(2,1)}, u32[]{:S(2)}) copy-start(bf16[1,320,1536]{2,1,0:T(8,128)(2,1)} %param.9) | copy-start | bytes 2949124
  7.2 63.8 %all-gather.5.cloned.1.call-start = ((), (), s32[]{:S(2)}) async-start(), calls=%async_computation | async-start | bytes 5898240 | tf_op jit(solution)/shard_map/all_gather | solution.py:77
  8.0 80.9 %all-gather.7.cloned.1.call-start = ((), (), s32[]{:S(2)}) async-start(), calls=%async_computation.1 | async-start | bytes 5898240 | tf_op jit(solution)/shard_map/all_gather | solution.py:78
  75.2 1.4 %copy-start.1 = (f32[320,1536]{1,0:T(8,128)}, f32[320,1536]{1,0:T(8,128)S(1)}, u32[]{:S(2)}) copy-start(f32[320,1536]{1,0:T(8,128)S(1)} %get-tuple-element.19) | copy-start | bytes 5898244
  76.6 12.3 %collective-permute-start.1 = (f32[1,1536]{1,0:T(1,128)S(1)}, f32[1,1536]{1,0:T(1,128)S(1)}, u32[]{:S(2)}, u32[]{:S(2)}) collective-permute-start(f32[1,1536]{1,0:T(1,128)S(1)} %slice.34), channel_id=1, source_target_pairs={{4,0},{8,4},{12,8},{16,12},{20,16},{24,20},{28,24},{5,1},{9,5},{13... | collective-permute-start | bytes 18440 | tf_op jit(solution)/shard_map/ppermute | solution.py:37
  78.1 15.0 %copy-start.9 = (f32[319,1536]{1,0:T(8,128)}, f32[319,1536]{1,0:T(8,128)S(1)}, u32[]{:S(2)}) copy-start(f32[319,1536]{1,0:T(8,128)S(1)} %slice.33) | copy-start | bytes 5879812
  93.1 1.3 copy-start.7
  93.1 6.1 %copy-start.2 = (f32[320,1536]{1,0:T(8,128)S(1)}, f32[320,1536]{1,0:T(8,128)}, u32[]{:S(2)}) copy-start(f32[320,1536]{1,0:T(8,128)} %copy-done.1) | copy-start | bytes 5898244
  94.3 4.9 %collective-permute-start = (f32[1,1536]{1,0:T(1,128)S(1)}, f32[1,1536]{1,0:T(1,128)S(1)}, u32[]{:S(2)}, u32[]{:S(2)}) collective-permute-start(f32[1,1536]{1,0:T(1,128)S(1)} %slice.31), channel_id=1, source_target_pairs={{0,4},{4,8},{8,12},{12,16},{16,20},{20,24},{24,28},{1,5},{5,9},{9,... | collective-permute-start | bytes 18440 | tf_op jit(solution)/shard_map/ppermute | solution.py:37
  99.2 1.2 copy-start.6
  101.6 0.9 copy-start.3
  103.1 4.0 %collective-permute-start.2 = (f32[1,1,1536]{2,1,0:T(1,128)S(1)}, f32[1,1,1536]{2,1,0:T(1,128)S(1)}, u32[]{:S(2)}, u32[]{:S(2)}) collective-permute-start(f32[1,1,1536]{2,1,0:T(1,128)S(1)} %broadcast_in_dim.69), channel_id=1, source_target_pairs={{0,4},{4,0},{8,12},{12,8},{16,20},{20,16},{24,28},{28,24},{1,5},{5... | collective-permute-start | bytes 18440 | tf_op jit(solution)/shard_map/ppermute | solution.py:23
  107.1 7.9 %collective-permute-start.3 = (f32[2,1,1536]{2,1,0:T(1,128)S(1)}, f32[2,1,1536]{2,1,0:T(1,128)S(1)}, u32[]{:S(2)}, u32[]{:S(2)}) collective-permute-start(f32[2,1,1536]{2,1,0:T(1,128)S(1)} %pad_maximum_fusion.4), channel_id=1, source_target_pairs={{0,8},{4,12},{8,0},{12,4},{16,24},{20,28},{24,16},{28,20},{1,9},{5... | collective-permute-start | bytes 36872 | tf_op jit(solution)/shard_map/ppermute | solution.py:23
  110.1 7.5 %copy-start.8 = (f32[320,1536]{1,0:T(8,128)S(1)}, f32[320,1536]{1,0:T(8,128)}, u32[]{:S(2)}) copy-start(f32[320,1536]{1,0:T(8,128)} %copy-done.7) | copy-start | bytes 5898244
  110.1 7.5 %copy-start.10 = (f32[319,1536]{1,0:T(8,128)S(1)}, f32[319,1536]{1,0:T(8,128)}, u32[]{:S(2)}) copy-start(f32[319,1536]{1,0:T(8,128)} %copy-done.9) | copy-start | bytes 5879812
  115.0 7.7 %collective-permute-start.4 = (f32[4,1,1536]{2,1,0:T(1,128)S(1)}, f32[4,1,1536]{2,1,0:T(1,128)S(1)}, u32[]{:S(2)}, u32[]{:S(2)}) collective-permute-start(f32[4,1,1536]{2,1,0:T(1,128)S(1)} %pad_maximum_fusion.3), channel_id=1, source_target_pairs={{0,16},{4,20},{8,24},{12,28},{16,0},{20,4},{24,8},{28,12},{1,17},{... | collective-permute-start | bytes 73736 | tf_op jit(solution)/shard_map/ppermute | solution.py:23
  117.5 6.1 %copy-start.4 = (f32[128,1536]{1,0:T(8,128)S(1)}, f32[128,1536]{1,0:T(8,128)}, u32[]{:S(2)}) copy-start(f32[128,1536]{1,0:T(8,128)} %copy-done.3) | copy-start | bytes 2359300
Sparse Core Ops, SparseCore 0:
  9.6 40.1 all-gather.4
  51.4 37.4 all-gather.6
